TPU v7x, 128 devices: a whole 4x4x4 slice. The times are simulated.
128 devices in a mesh: dp: 16 (over x, y), head: 8 (over z, core).
Axes of the slice: x: 4, y: 4, z: 4, core: 2. Of those that a mesh axis runs over, the one named last changes fastest.
Arguments:
- tokens: bfloat16 [16384, 2048], P(('dp', 'head')), may hold values from -6 to 6
- cached_lens: int32 [16], replicated, may hold values from 1 to 2048, as said below
- latent_cache: bfloat16 [16, 2048, 576], P(None, 'dp'), may hold values from -720 to 720
- attn_gain: float32 [2048], replicated, may hold values from 0.1 to 1.9
- q_weight: bfloat16 [2048, 3072], P(None, 'head'), may hold values from -0.125 to 0.125
- kv_down: bfloat16 [2048, 576], replicated, may hold values from -0.125 to 0.125
- latent_gain: float32 [512], replicated, may hold values from 0.1 to 1.9
- kv_up: bfloat16 [512, 4096], P(None, 'head'), may hold values from -1 to 1
- o_weight: bfloat16 [2048, 2048], P('head'), may hold values from -0.125 to 0.125
- moe_gain: float32 [2048], replicated, may hold values from 0.1 to 1.9
- routes: int32 [16384, 6], P(('dp', 'head')), may hold values from 0 to 63, all different within a row; in each aligned block of 128 rows (0 to 127, 128 to 255, ...) at most 16 rows name the same one
- route_weights: float32 [16384, 6], P(('dp', 'head')), may hold values from 0.1 to 1
- expert_gate_up: bfloat16 [128, 2048, 1408], P(('dp', 'head')), may hold values from -0.125 to 0.125
- expert_down: bfloat16 [128, 704, 2048], P(('dp', 'head')), may hold values from -0.15625 to 0.15625
Outputs:
- layer_out: bfloat16 [16384, 2048], P(('dp', 'head'))
Inputs may be any that keep to these rules, and one draw needn't show every extreme that they name: `cached_lens`: one request's cached length is exactly 2048. `routes`: each token names 6 different experts; among the rows of one device (aligned blocks of 128 tokens) no expert is named more than 16 times, a bound that some block reaches.
All inputs are finite; a program needn't handle non-finite values.
Results may differ from a plain program's by a relative error of at most 0.019.
The roundings to bfloat16 on the way count: a program that leaves them out, or rounds other values in their place, can miss the bound.
Values may be sent and summed in bfloat16 or wider, within the bound.
No kernel may reach another device: no remote copies, remote signals or barrier semaphores. Data moves between devices by JAX's collectives and lax.ppermute only.
A program may use at most 128 MiB of HBM per device.

v0:
```python
import jax
import jax.numpy as jnp
import numpy as np
from jax import lax
from jax.experimental import pallas as pl
from jax.experimental.pallas import tpu as pltpu
from jax.sharding import PartitionSpec as P

D = 2048
HN = 128
HR = 64
HV = 128
LAT = 512
EXPERTS = 64
TOPK = 6
CAP = 16
HALF = 704
HEAD = ("z", "core")
ROWS = ("dp", "z", "core")


NORM_EPS = 1e-06


def norm_rows(values, gain_row):
    return (
        values * lax.rsqrt(jnp.mean(values * values, axis=-1, keepdims=True) + NORM_EPS) * gain_row
    )


def angle_table(positions):
    half_width = HR // 2
    inverse = np.exp(np.arange(half_width) * (-np.log(10000.0) / half_width)).astype(np.float32)
    return positions.astype(jnp.float32)[:, None] * jnp.asarray(inverse, dtype=jnp.float32)[None, :]


def rotate_pair(values, angles):
    half_width = values.shape[-1] // 2
    cosine = jnp.cos(angles)
    sine_part = jnp.sin(angles)
    former = values[..., :half_width]
    latter = values[..., half_width:]
    return jnp.concatenate(
        [former * cosine - latter * sine_part, latter * cosine + former * sine_part], axis=-1
    )


def query_rows(normed, q_weight, positions):
    mixed_rows = jnp.dot(normed, q_weight, preferred_element_type=jnp.float32)
    head_count = q_weight.shape[1] // (HN + HR)
    mixed_rows = mixed_rows.reshape(normed.shape[0], head_count, HN + HR)
    turned = rotate_pair(mixed_rows[:, :, HN:], angle_table(positions)[:, None, :])
    joined = jnp.concatenate([mixed_rows[:, :, :HN], turned], axis=2)
    return joined.reshape(normed.shape[0], head_count * (HN + HR)).astype(jnp.bfloat16)


def expand_rows(key_rows, kv_up):
    return jnp.dot(key_rows[:, :LAT], kv_up, preferred_element_type=jnp.float32).astype(
        jnp.bfloat16
    )


Q_BLOCK = 128


def attend_kernel(qn_ref, qr_ref, *refs):
    o_ref = refs[-1]
    parts = [refs[i : i + 3] for i in range(0, len(refs) - 1, 3)]
    heads = qr_ref.shape[0]
    first = pl.program_id(0) * Q_BLOCK
    q_idx = first + lax.broadcasted_iota(jnp.int32, (Q_BLOCK, 1), 0)
    contract = (((1,), (1,)), ((), ()))

    def one_head(h, carry):
        qn = qn_ref[:, pl.ds(pl.multiple_of(h * HN, HN), HN)]
        qr = qr_ref[h]
        scores = []
        for kw_ref, kr_ref, th_ref in parts:
            kn = kw_ref[:, pl.ds(pl.multiple_of(h * (HN + HV), HN + HV), HN)]
            part = lax.dot_general(qn, kn, contract, preferred_element_type=jnp.float32)
            part = part + lax.dot_general(
                qr, kr_ref[...], contract, preferred_element_type=jnp.float32
            )
            part = part * (HN + HR) ** (-0.5)
            scores.append(jnp.where(q_idx >= th_ref[...], part, -1e30))
        row_max = scores[0].max(axis=1, keepdims=True)
        for part in scores[1:]:
            row_max = jnp.maximum(row_max, part.max(axis=1, keepdims=True))
        weights = []
        for part, (kw_ref, kr_ref, th_ref) in zip(scores, parts):
            weights.append(jnp.where(q_idx >= th_ref[...], jnp.exp(part - row_max), 0.0))
        total = weights[0].sum(axis=1, keepdims=True)
        for part in weights[1:]:
            total = total + part.sum(axis=1, keepdims=True)
        mixed = jnp.zeros((Q_BLOCK, HV), jnp.float32)
        for part, (kw_ref, kr_ref, th_ref) in zip(weights, parts):
            vals = kw_ref[:, pl.ds(pl.multiple_of(h * (HN + HV) + HN, HN), HV)]
            mixed = mixed + jnp.dot(
                (part / total).astype(jnp.bfloat16), vals, preferred_element_type=jnp.float32
            )
        o_ref[:, pl.ds(pl.multiple_of(h * HV, HV), HV)] = mixed.astype(jnp.bfloat16)
        return carry

    lax.fori_loop(0, heads, one_head, 0)


def attend_all(q_nope, q_rope, key_parts, interpret=False):
    span, nope_width = q_nope.shape
    heads = q_rope.shape[0]
    in_specs = [
        pl.BlockSpec((Q_BLOCK, nope_width), lambda i: (i, 0)),
        pl.BlockSpec((heads, Q_BLOCK, HR), lambda i: (0, i, 0)),
    ]
    operands = [q_nope, q_rope]
    for key_wide, rope_keys, thresh in key_parts:
        keys = key_wide.shape[0]
        in_specs += [
            pl.BlockSpec((keys, key_wide.shape[1]), lambda i: (0, 0)),
            pl.BlockSpec((keys, HR), lambda i: (0, 0)),
            pl.BlockSpec((1, keys), lambda i: (0, 0)),
        ]
        operands += [key_wide, rope_keys, thresh]
    return pl.pallas_call(
        attend_kernel,
        grid=(span // Q_BLOCK,),
        in_specs=in_specs,
        out_specs=pl.BlockSpec((Q_BLOCK, heads * HV), lambda i: (i, 0)),
        out_shape=jax.ShapeDtypeStruct((span, heads * HV), jnp.bfloat16),
        compiler_params=pltpu.CompilerParams(
            dimension_semantics=("arbitrary",), vmem_limit_bytes=48 * 1024 * 1024
        ),
        interpret=interpret,
    )(*operands)


def expert_half(rows, gate_up, down):
    mixed_rows = jnp.dot(rows, gate_up, preferred_element_type=jnp.float32)
    active = (jax.nn.silu(mixed_rows[:, :HALF]) * mixed_rows[:, HALF:]).astype(jnp.bfloat16)
    return (
        jnp.dot(active, down, preferred_element_type=jnp.float32)
        .astype(jnp.bfloat16)
        .astype(jnp.float32)
    )


def layer_body(
    tokens,
    cached_lens,
    latent_cache,
    attn_gain,
    q_weight,
    kv_down,
    latent_gain,
    kv_up,
    o_weight,
    moe_gain,
    routes,
    route_weights,
    expert_gate_up,
    expert_down,
):
    head_count = lax.axis_size("z") * lax.axis_size("core")
    swap = [(0, 1), (1, 0)]
    other_gate_up = lax.ppermute(expert_gate_up, "core", swap)
    other_down = lax.ppermute(expert_down, "core", swap)
    request = lax.axis_index("dp")
    own_rows = tokens.shape[0]
    span_len = own_rows * head_count
    length = lax.dynamic_index_in_dim(cached_lens, request, 0, keepdims=False)
    local_heads = q_weight.shape[1] // (HN + HR)
    normed = norm_rows(tokens.astype(jnp.float32), attn_gain).astype(jnp.bfloat16)
    shard_rows = lax.all_gather(normed, HEAD, axis=0, tiled=True)
    o_src, shard_rows = lax.optimization_barrier((o_weight, shard_rows))
    o_full = lax.all_gather(o_src, HEAD, axis=0, tiled=True)
    positions = length + jnp.arange(shard_rows.shape[0], dtype=jnp.int32)
    queries = query_rows(shard_rows, q_weight, positions)
    fresh_mixed = jnp.dot(shard_rows, kv_down, preferred_element_type=jnp.float32)
    fresh_latent = norm_rows(fresh_mixed[:, :LAT], latent_gain).astype(jnp.bfloat16)
    fresh_rope = rotate_pair(fresh_mixed[:, LAT:], angle_table(positions)).astype(jnp.bfloat16)
    core = lax.axis_index("core")
    quarter = latent_cache.shape[1] // 2
    cache_part = lax.dynamic_slice_in_dim(latent_cache, core * quarter, quarter, 1)
    mine = lax.all_to_all(
        cache_part,
        "dp",
        split_axis=0,
        concat_axis=1,
        tiled=True,
    )[0]
    theirs = lax.ppermute(mine, "core", swap)
    cache_rows = jnp.arange(mine.shape[0], dtype=jnp.int32)
    cache_pos = cache_rows // quarter * (2 * quarter) + cache_rows % quarter
    fresh_pos = jnp.arange(span_len, dtype=jnp.int32)

    def cache_thresh(pos):
        return jnp.where(pos < length, -1, 1 << 30).reshape(1, -1)

    key_parts = (
        (expand_rows(mine, kv_up), mine[:, LAT:], cache_thresh(cache_pos + core * quarter)),
        (
            expand_rows(theirs, kv_up),
            theirs[:, LAT:],
            cache_thresh(cache_pos + (1 - core) * quarter),
        ),
        (expand_rows(fresh_latent, kv_up), fresh_rope, fresh_pos.reshape(1, -1)),
    )
    query_heads = queries.reshape(span_len, local_heads, HN + HR)
    heads_out = attend_all(
        query_heads[:, :, :HN].reshape(span_len, local_heads * HN),
        query_heads[:, :, HN:].transpose(1, 0, 2),
        key_parts,
    )
    heads_mine = lax.all_to_all(heads_out, HEAD, split_axis=0, concat_axis=1, tiled=True)
    group_terms = jnp.einsum(
        "tgc,gcd->gtd",
        heads_mine.reshape(own_rows, head_count, -1),
        o_full.reshape(head_count, -1, D),
        preferred_element_type=jnp.float32,
    )
    attn_out = jnp.sum(group_terms.astype(jnp.bfloat16).astype(jnp.float32), axis=0)
    hidden = tokens.astype(jnp.float32) + attn_out
    moe_in = norm_rows(hidden, moe_gain).astype(jnp.bfloat16)
    flat_routes = routes.reshape(-1)
    onehot = (flat_routes[:, None] == jnp.arange(EXPERTS, dtype=jnp.int32)[None, :]).astype(
        jnp.int32
    )
    rank_ids = jnp.sum((jnp.cumsum(onehot, axis=0) - onehot) * onehot, axis=1)
    slot_tk = (flat_routes * CAP + rank_ids).reshape(own_rows, TOPK)
    slot_iota = jnp.arange(EXPERTS * CAP, dtype=jnp.int32)
    dispatch = jnp.any(slot_tk[None, :, :] == slot_iota[:, None, None], axis=2).astype(
        jnp.bfloat16
    )
    outgoing = jnp.dot(dispatch, moe_in, preferred_element_type=jnp.float32).astype(jnp.bfloat16)
    outgoing = outgoing.reshape(EXPERTS, CAP, D)
    pieces = []
    for chunk in range(2):
        part = CAP // 2
        arrived = lax.all_to_all(
            outgoing[:, chunk * part : (chunk + 1) * part],
            ("dp", "z"),
            split_axis=0,
            concat_axis=0,
            tiled=True,
        ).reshape(EXPERTS * part, D)
        total = expert_half(arrived, expert_gate_up[0], expert_down[0]) + expert_half(
            arrived, other_gate_up[0], other_down[0]
        )
        pieces.append(
            lax.all_to_all(
                total.astype(jnp.bfloat16).reshape(EXPERTS, part, D),
                ("dp", "z"),
                split_axis=0,
                concat_axis=0,
                tiled=True,
            )
        )
    returned = jnp.concatenate(pieces, axis=1).reshape(EXPERTS * CAP, D)
    slot_weights = jnp.sum(
        jnp.where(slot_tk[:, :, None] == slot_iota[None, None, :], route_weights[:, :, None], 0.0),
        axis=1,
    )
    weights_hi = slot_weights.astype(jnp.bfloat16)
    weights_lo = (slot_weights - weights_hi.astype(jnp.float32)).astype(jnp.bfloat16)
    routed_out = jnp.dot(weights_hi, returned, preferred_element_type=jnp.float32) + jnp.dot(
        weights_lo, returned, preferred_element_type=jnp.float32
    )
    return (hidden + routed_out).astype(jnp.bfloat16)


def solution(mesh):
    chips = jax.sharding.Mesh(
        mesh.devices.reshape(mesh.shape["dp"], -1, 2), ("dp", "z", "core")
    )
    placed = (
        P(ROWS, None),
        P(),
        P(None, "dp", None),
        P(),
        P(None, HEAD),
        P(),
        P(),
        P(None, HEAD),
        P(HEAD, None),
        P(),
        P(ROWS, None),
        P(ROWS, None),
        P(ROWS, None, None),
        P(ROWS, None, None),
    )
    return jax.shard_map(
        layer_body, mesh=chips, in_specs=placed, out_specs=P(ROWS, None), check_vma=False
    )
```

profile of v0, /device:TPU:0, one launch (start us, length us, event | category | flops | bytes accessed | tf_op | source)
XLA Modules:
  0.0 312.0 jit_solution(2908940230281743622)
XLA Ops:
  6.5 1.4 fusion.33
  7.9 2.0 fusion.35
  10.0 34.9 %all-gather.3.cloned.1.call-done = bf16[1024,2048]{1,0:T(8,128)(2,1)} async-done(((bf16[128,2048]{1,0:T(8,128)(2,1)}), bf16[1024,2048]{1,0:T(8,128)(2,1)}) %all-gather.3.cloned.1.call-update) | async-done | bytes 4194320 | tf_op jit(solution)/shard_map/all_gather | solution.py:172
  44.9 2.2 constant_dynamic-slice_fusion
  47.1 3.8 %copy.79 = bf16[16,64,576]{2,1,0:T(8,128)(2,1)} copy(bf16[16,64,576]{1,2,0:T(8,128)(2,1)} %constant_dynamic-slice_fusion) | data formatting | bytes 2359296
  51.0 27.1 %all_to_all.45 = bf16[16,64,576]{2,1,0:T(8,128)(2,1)S(1)} all-to-all(bf16[16,64,576]{2,1,0:T(8,128)(2,1)} %copy.79), channel_id=1, replica_groups=mesh['dp'=16,'z'=4,'core'=2] {'dp'}, dimensions={0} | all-to-all | bytes 2359296 | tf_op jit(solution)/shard_map/all_to_all | solution.py:183
  79.7 1.8 reduce-window.6
  83.8 2.0 convolution_convert_fusion.7.refs_0_
  85.8 0.9 slice.104
  86.9 2.2 convolution_convert_fusion.6.refs_3_
  89.1 4.6 %fusion.68 = f32[1024,576]{0,1:T(8,128)S(1)} fusion(bf16[1024,2048]{1,0:T(8,128)(2,1)} %all-gather.3.cloned.1.call-done, bf16[2048,576]{0,1:T(8,128)(2,1)S(1)} %copy-done.20), kind=kOutput, calls=%fused_computation.111 | convolution fusion | flops 2415919104 | bytes 8912896 | tf_op jit(solution)/shard_map/dot_general | solution.py:177
  93.7 1.4 copy-done.8
  95.1 1.0 copy.81
  96.1 1.0 copy.82
  97.2 4.5 %fusion.67 = f32[1024,384]{0,1:T(8,128)S(1)} fusion(bf16[1024,2048]{1,0:T(8,128)(2,1)} %all-gather.3.cloned.1.call-done, bf16[2048,384]{1,0:T(8,128)(2,1)} %param.20), kind=kOutput, calls=%fused_computation.110 | convolution fusion | flops 1610612736 | bytes 7340032 | tf_op jit(solution)/shard_map/dot_general | solution.py:49
  101.7 0.9 slice.152
  102.6 1.3 copy.77
  103.9 1.3 copy.78
  105.2 1.2 copy.72.qn_ref
  106.5 3.9 %subtract_convert_fusion.2 = (bf16[1024,32]{1,0:T(8,128)(2,1)S(1)}, bf16[1024,32]{1,0:T(8,128)(2,1)S(1)}, f32[1024,32]{1,0:T(8,128)S(1)}, f32[1024,32]{1,0:T(8,128)S(1)}) fusion(f32[1024,32]{1,0:T(8,128)} %copy.82, f32[1024,32]{1,0:T(8,128)} %copy.81, f32[1024]{0:T(1024)S(1)} %add_convert_fusion.4, f32[32]{0:T(128)S(1)} %copy-done.17), kind=kLoop, calls=%fused_computation.74 | loop fusion | flops 294912 | bytes 659584 | tf_op jit(solution)/shard_map/convert
  111.2 1.0 copy-done.9
  113.3 22.9 %shard_map.154 = bf16[1024,256]{1,0:T(8,128)(2,1)} custom-call(bf16[1024,256]{1,0:T(8,128)(2,1)S(1)} %copy.72.qn_ref, bf16[2,1024,64]{2,1,0:T(8,128)(2,1)S(1)} %maximum_bitcast_fusion.qr_ref, bf16[1024,512]{1,0:T(8,128)(2,1)S(1)} %convolution_convert_fusion.7.refs_0_, bf16[1024,64]{1,0:T(8,128)(2,1)S(1)} %slice.102.refs_1_, ...), custom_call_target="tpu_custom_call" | custom-call | tf_op jit(solution)/shard_map/pallas_call | solution.py:123
  136.2 3.7 %all-to-all-start.1 = ((bf16[8,128,256]{2,1,0:T(8,128)(2,1)}), bf16[8,128,256]{2,1,0:T(8,128)(2,1)S(1)}, u32[]{:S(2)}, u32[]{:S(2)}) async-start(bf16[8,128,256]{2,1,0:T(8,128)(2,1)} %bitcast.5), calls=%async_computation.1 | async-start | bytes 1048576 | tf_op jit(solution)/shard_map/all_to_all | solution.py:213
  140.8 9.4 %all-to-all-done.1 = bf16[8,128,256]{2,1,0:T(8,128)(2,1)S(1)} async-done(((bf16[8,128,256]{2,1,0:T(8,128)(2,1)}), bf16[8,128,256]{2,1,0:T(8,128)(2,1)S(1)}, u32[]{:S(2)}, u32[]{:S(2)}) %all-to-all-start.1) | async-done | bytes 524320 | tf_op jit(solution)/shard_map/all_to_all | solution.py:213
  150.2 4.7 %convert_reduce_fusion = f32[128,2048]{1,0:T(8,128)S(1)} fusion(bf16[8,256,2048]{2,1,0:T(8,128)(2,1)} %bitcast.89, bf16[8,128,256]{2,1,0:T(8,128)(2,1)S(1)} %all-to-all-done.1), kind=kOutput, calls=%fused_computation | convolution fusion | flops 1079771136 | bytes 9961472 | tf_op jit(solution)/shard_map/tgc,gcd->gtd/dot_general | solution.py:214
  155.2 1.3 convolution_convert_fusion
  156.5 2.5 fusion.64
  159.0 5.2 %all-to-all-start.2 = ((bf16[64,8,2048]{2,1,0:T(8,128)(2,1)}), bf16[64,8,2048]{2,1,0:T(8,128)(2,1)S(1)}, u32[]{:S(2)}, u32[]{:S(2)}) async-start(bf16[64,8,2048]{2,1,0:T(8,128)(2,1)} %get-tuple-element.9), calls=%async_computation.2 | async-start | bytes 4194304 | tf_op jit(solution)/shard_map/all_to_all | solution.py:238
  164.3 29.3 %all-to-all-done.2 = bf16[64,8,2048]{2,1,0:T(8,128)(2,1)S(1)} async-done(((bf16[64,8,2048]{2,1,0:T(8,128)(2,1)}), bf16[64,8,2048]{2,1,0:T(8,128)(2,1)S(1)}, u32[]{:S(2)}, u32[]{:S(2)}) %all-to-all-start.2) | async-done | bytes 2097184 | tf_op jit(solution)/shard_map/all_to_all | solution.py:238
  193.6 1.3 copy-done.12
  195.0 5.2 %all-to-all-start.4 = ((bf16[64,8,2048]{2,1,0:T(8,128)(2,1)}), bf16[64,8,2048]{2,1,0:T(8,128)(2,1)S(1)}, u32[]{:S(2)}, u32[]{:S(2)}) async-start(bf16[64,8,2048]{2,1,0:T(8,128)(2,1)} %get-tuple-element.10), calls=%async_computation.4 | async-start | bytes 4194304 | tf_op jit(solution)/shard_map/all_to_all | solution.py:238
  200.2 6.5 %fusion.6 = f32[512,1408]{1,0:T(8,128)S(1)} fusion(bf16[1,2048,1408]{2,1,0:T(8,128)(2,1)} %param.28, bf16[64,8,2048]{2,1,0:T(8,128)(2,1)} %copy-done.12), kind=kOutput, calls=%fused_computation.7 | convolution fusion | flops 2952790016 | bytes 10747904 | tf_op jit(solution)/shard_map/dot_general | solution.py:137
  206.8 1.9 convolution_convert_fusion.4
  208.7 5.7 %fusion.2 = f32[512,1408]{1,0:T(8,128)S(1)} fusion(bf16[1,2048,1408]{2,1,0:T(8,128)(2,1)} %collective-permute-done.1, bf16[64,8,2048]{2,1,0:T(8,128)(2,1)S(1)} %copy-done.13), kind=kOutput, calls=%fused_computation.3 | convolution fusion | flops 2952790016 | bytes 10747904 | tf_op jit(solution)/shard_map/dot_general | solution.py:137
  214.4 5.0 %fusion.15 = bf16[64,8,2048]{2,1,0:T(8,128)(2,1)} fusion(bf16[1,704,2048]{2,1,0:T(8,128)(2,1)} %collective-permute-done.2, bf16[512,2048]{1,0:T(8,128)(2,1)S(1)} %convolution_convert_fusion.4, f32[512,1408]{1,0:T(8,128)S(1)} %fusion.2), kind=kOutput, calls=%fused_computation.25 | convolution fusion | flops 1483800576 | bytes 10223616 | tf_op jit(solution)/shard_map/dot_general | solution.py:140
  219.5 10.1 %all-to-all-done.4 = bf16[64,8,2048]{2,1,0:T(8,128)(2,1)S(1)} async-done(((bf16[64,8,2048]{2,1,0:T(8,128)(2,1)}), bf16[64,8,2048]{2,1,0:T(8,128)(2,1)S(1)}, u32[]{:S(2)}, u32[]{:S(2)}) %all-to-all-start.4) | async-done | bytes 2097184 | tf_op jit(solution)/shard_map/all_to_all | solution.py:238
  229.6 1.4 copy-done.10
  231.0 5.4 %all-to-all-start.3 = ((bf16[64,8,2048]{2,1,0:T(8,128)(2,1)}), bf16[64,8,2048]{2,1,0:T(8,128)(2,1)S(1)}, u32[]{:S(2)}, u32[]{:S(2)}) async-start(bf16[64,8,2048]{2,1,0:T(8,128)(2,1)} %fusion.15), calls=%async_computation.3 | async-start | bytes 4194304 | tf_op jit(solution)/shard_map/all_to_all | solution.py:249
  236.4 6.5 %fusion.4 = f32[512,1408]{1,0:T(8,128)S(1)} fusion(bf16[1,2048,1408]{2,1,0:T(8,128)(2,1)} %param.28, bf16[64,8,2048]{2,1,0:T(8,128)(2,1)} %copy-done.10), kind=kOutput, calls=%fused_computation.5 | convolution fusion | flops 2952790016 | bytes 10747904 | tf_op jit(solution)/shard_map/dot_general | solution.py:137
  243.0 1.9 convolution_convert_fusion.2
  244.9 5.8 %fusion = f32[512,1408]{1,0:T(8,128)S(1)} fusion(bf16[1,2048,1408]{2,1,0:T(8,128)(2,1)} %collective-permute-done.1, bf16[64,8,2048]{2,1,0:T(8,128)(2,1)S(1)} %copy-done.11), kind=kOutput, calls=%fused_computation.1 | convolution fusion | flops 2952790016 | bytes 10747904 | tf_op jit(solution)/shard_map/dot_general | solution.py:137
  250.7 5.1 %fusion.20 = bf16[64,8,2048]{2,1,0:T(8,128)(2,1)} fusion(bf16[1,704,2048]{2,1,0:T(8,128)(2,1)} %collective-permute-done.2, bf16[512,2048]{1,0:T(8,128)(2,1)S(1)} %convolution_convert_fusion.2, f32[512,1408]{1,0:T(8,128)S(1)} %fusion), kind=kOutput, calls=%fused_computation.26 | convolution fusion | flops 1483800576 | bytes 10223616 | tf_op jit(solution)/shard_map/dot_general | solution.py:140
  255.7 9.9 %all-to-all-done.3 = bf16[64,8,2048]{2,1,0:T(8,128)(2,1)S(1)} async-done(((bf16[64,8,2048]{2,1,0:T(8,128)(2,1)}), bf16[64,8,2048]{2,1,0:T(8,128)(2,1)S(1)}, u32[]{:S(2)}, u32[]{:S(2)}) %all-to-all-start.3) | async-done | bytes 2097184 | tf_op jit(solution)/shard_map/all_to_all | solution.py:249
  265.7 5.6 %all-to-all-start.5 = ((bf16[64,8,2048]{2,1,0:T(8,128)(2,1)}), bf16[64,8,2048]{2,1,0:T(8,128)(2,1)}, u32[]{:S(2)}, u32[]{:S(2)}) async-start(bf16[64,8,2048]{2,1,0:T(8,128)(2,1)} %fusion.20), calls=%async_computation.5 | async-start | bytes 4194304 | tf_op jit(solution)/shard_map/all_to_all | solution.py:249
  271.2 1.2 select_reduce_fusion
  272.5 28.0 %all-to-all-done.5 = bf16[64,8,2048]{2,1,0:T(8,128)(2,1)} async-done(((bf16[64,8,2048]{2,1,0:T(8,128)(2,1)}), bf16[64,8,2048]{2,1,0:T(8,128)(2,1)}, u32[]{:S(2)}, u32[]{:S(2)}) %all-to-all-start.5) | async-done | bytes 2097184 | tf_op jit(solution)/shard_map/all_to_all | solution.py:249
  300.5 2.0 pad_maximum_fusion
  303.5 1.7 fusion.24
  (87 shorter events, 8.2 us)
Async XLA Ops:
  6.5 38.4 %copy-start = (bf16[16,128,576]{1,2,0:T(8,128)(2,1)S(1)}, bf16[16,128,576]{1,2,0:T(8,128)(2,1)}, u32[]{:S(2)}) copy-start(bf16[16,128,576]{1,2,0:T(8,128)(2,1)} %param.18) | copy-start | bytes 7077892
  6.5 38.4 %all-gather.3.cloned.1.call-start = ((), (), s32[]{:S(2)}) async-start(), calls=%async_computation.6 | async-start | bytes 4718592 | tf_op jit(solution)/shard_map/all_gather | solution.py:172
  10.0 140.2 %all-gather.5.cloned.1.call-start = ((), (), s32[]{:S(2)}) async-start(), calls=%async_computation.7 | async-start | bytes 9437184 | tf_op jit(solution)/shard_map/all_gather | solution.py:174
  51.0 28.3 %copy-start.14 = (s32[128,6]{0,1:T(8,128)S(1)}, s32[128,6]{0,1:T(8,128)}, u32[]{:S(2)}) copy-start(s32[128,6]{0,1:T(8,128)} %param.26) | copy-start | bytes 9220
  78.0 5.7 %copy-start.4 = (bf16[16,64,576]{2,1,0:T(8,128)(2,1)}, bf16[16,64,576]{2,1,0:T(8,128)(2,1)S(1)}, u32[]{:S(2)}) copy-start(bf16[16,64,576]{2,1,0:T(8,128)(2,1)S(1)} %all_to_all.45) | copy-start | bytes 3538948
  78.0 3.7 %copy-start.24 = (s32[16]{0:T(128)S(1)}, s32[16]{0:T(128)}, u32[]{:S(2)}) copy-start(s32[16]{0:T(128)} %param.17) | copy-start | bytes 196
  78.0 5.7 %copy-start.21 = (bf16[512,512]{1,0:T(8,128)(2,1)S(1)}, bf16[512,512]{1,0:T(8,128)(2,1)}, u32[]{:S(2)}) copy-start(bf16[512,512]{1,0:T(8,128)(2,1)} %param.23) | copy-start | bytes 1572868
  78.7 7.1 %collective-permute-start = (bf16[1024,576]{0,1:T(8,128)(2,1)S(1)}, bf16[1024,576]{0,1:T(8,128)(2,1)}, u32[]{:S(2)}, u32[]{:S(2)}) collective-permute-start(bf16[1024,576]{0,1:T(8,128)(2,1)S(1)} %copy.68), channel_id=1, source_target_pairs={{0,1},{1,0},{2,3},{3,2},{4,5},{5,4},{6,7},{7,6},{8,9},{9,8},{10,11... | collective-permute-start | bytes 3538952 | tf_op jit(solution)/shard_map/ppermute | solution.py:190
  78.8 129.9 %collective-permute-start.1 = (bf16[1,2048,1408]{2,1,0:T(8,128)(2,1)}, bf16[1,2048,1408]{2,1,0:T(8,128)(2,1)}, u32[]{:S(2)}, u32[]{:S(2)}) collective-permute-start(bf16[1,2048,1408]{2,1,0:T(8,128)(2,1)} %param.28), channel_id=1, source_target_pairs={{0,1},{1,0},{2,3},{3,2},{4,5},{5,4},{6,7},{7,6},{8,9},{9,8},{10,11... | collective-permute-start | bytes 17301512 | tf_op jit(solution)/shard_map/ppermute | solution.py:164
  86.8 2.3 copy-start.20
  93.7 1.4 copy-start.8
  102.5 3.9 %copy-start.17 = (f32[32]{0:T(128)S(1)}, f32[32]{0:T(128)}, u32[]{:S(2)}) copy-start(f32[32]{0:T(128)} %constant.83.clone) | copy-start | bytes 388
  106.5 4.1 %copy-start.6 = (f32[1024,2,32]{2,0,1:T(8,128)S(1)}, f32[1024,2,32]{2,0,1:T(8,128)}, u32[]{:S(2)}) copy-start(f32[1024,2,32]{2,0,1:T(8,128)} %copy.77) | copy-start | bytes 786436
  106.5 4.1 %copy-start.7 = (f32[1024,2,32]{2,0,1:T(8,128)S(1)}, f32[1024,2,32]{2,0,1:T(8,128)}, u32[]{:S(2)}) copy-start(f32[1024,2,32]{2,0,1:T(8,128)} %copy.78) | copy-start | bytes 786436
  110.6 1.7 copy-start.9
  110.9 1.6 copy-start.22
  110.9 1.6 copy-start.23
  136.2 13.9 %all-to-all-start.1 = ((bf16[8,128,256]{2,1,0:T(8,128)(2,1)}), bf16[8,128,256]{2,1,0:T(8,128)(2,1)S(1)}, u32[]{:S(2)}, u32[]{:S(2)}) async-start(bf16[8,128,256]{2,1,0:T(8,128)(2,1)} %bitcast.5), calls=%async_computation.1 | async-start | bytes 1048576 | tf_op jit(solution)/shard_map/all_to_all | solution.py:213
  150.1 4.8 %copy-start.2 = (bf16[128,2048]{1,0:T(8,128)(2,1)S(1)}, bf16[128,2048]{1,0:T(8,128)(2,1)}, u32[]{:S(2)}) copy-start(bf16[128,2048]{1,0:T(8,128)(2,1)} %param.16) | copy-start | bytes 1572868
  150.1 5.0 %copy-start.15 = (f32[2048]{0:T(1024)S(1)}, f32[2048]{0:T(1024)}, u32[]{:S(2)}) copy-start(f32[2048]{0:T(1024)} %param.25) | copy-start | bytes 24580
  159.0 34.6 %all-to-all-start.2 = ((bf16[64,8,2048]{2,1,0:T(8,128)(2,1)}), bf16[64,8,2048]{2,1,0:T(8,128)(2,1)S(1)}, u32[]{:S(2)}, u32[]{:S(2)}) async-start(bf16[64,8,2048]{2,1,0:T(8,128)(2,1)} %get-tuple-element.9), calls=%async_computation.2 | async-start | bytes 4194304 | tf_op jit(solution)/shard_map/all_to_all | solution.py:238
  164.2 50.2 %collective-permute-start.2 = (bf16[1,704,2048]{2,1,0:T(8,128)(2,1)}, bf16[1,704,2048]{2,1,0:T(8,128)(2,1)}, u32[]{:S(2)}, u32[]{:S(2)}) collective-permute-start(bf16[1,704,2048]{2,1,0:T(8,128)(2,1)} %param.29), channel_id=1, source_target_pairs={{0,1},{1,0},{2,3},{3,2},{4,5},{5,4},{6,7},{7,6},{8,9},{9,8},{10,11... | collective-permute-start | bytes 8650760 | tf_op jit(solution)/shard_map/ppermute | solution.py:165
  193.6 1.3 copy-start.12
  195.0 34.6 %all-to-all-start.4 = ((bf16[64,8,2048]{2,1,0:T(8,128)(2,1)}), bf16[64,8,2048]{2,1,0:T(8,128)(2,1)S(1)}, u32[]{:S(2)}, u32[]{:S(2)}) async-start(bf16[64,8,2048]{2,1,0:T(8,128)(2,1)} %get-tuple-element.10), calls=%async_computation.4 | async-start | bytes 4194304 | tf_op jit(solution)/shard_map/all_to_all | solution.py:238
  200.2 6.6 %copy-start.18 = (bf16[1,704,2048]{2,1,0:T(8,128)(2,1)S(1)}, bf16[1,704,2048]{2,1,0:T(8,128)(2,1)}, u32[]{:S(2)}) copy-start(bf16[1,704,2048]{2,1,0:T(8,128)(2,1)} %param.29) | copy-start | bytes 8650756
  206.7 1.9 copy-start.13
  229.6 1.4 copy-start.10
  231.0 34.7 %all-to-all-start.3 = ((bf16[64,8,2048]{2,1,0:T(8,128)(2,1)}), bf16[64,8,2048]{2,1,0:T(8,128)(2,1)S(1)}, u32[]{:S(2)}, u32[]{:S(2)}) async-start(bf16[64,8,2048]{2,1,0:T(8,128)(2,1)} %fusion.15), calls=%async_computation.3 | async-start | bytes 4194304 | tf_op jit(solution)/shard_map/all_to_all | solution.py:249
  236.4 6.6 %copy-start.19 = (bf16[1,704,2048]{2,1,0:T(8,128)(2,1)S(1)}, bf16[1,704,2048]{2,1,0:T(8,128)(2,1)}, u32[]{:S(2)}) copy-start(bf16[1,704,2048]{2,1,0:T(8,128)(2,1)} %param.29) | copy-start | bytes 8650756
  243.0 1.9 copy-start.11
  255.7 15.5 %copy-start.16 = (f32[128,6]{0,1:T(8,128)S(1)}, f32[128,6]{0,1:T(8,128)}, u32[]{:S(2)}) copy-start(f32[128,6]{0,1:T(8,128)} %param.27) | copy-start | bytes 9220
  265.7 34.8 %all-to-all-start.5 = ((bf16[64,8,2048]{2,1,0:T(8,128)(2,1)}), bf16[64,8,2048]{2,1,0:T(8,128)(2,1)}, u32[]{:S(2)}, u32[]{:S(2)}) async-start(bf16[64,8,2048]{2,1,0:T(8,128)(2,1)} %fusion.20), calls=%async_computation.5 | async-start | bytes 4194304 | tf_op jit(solution)/shard_map/all_to_all | solution.py:249
  300.5 2.0 copy-start.5
  302.4 1.0 copy-start.3
  302.4 2.8 copy-start.1
Sparse Core Ops, SparseCore 0:
  10.1 34.7 all-gather.2
  46.6 49.6 all-gather.4
where the time goes:
time: 313 us; the launch traced here: 312 us
  waiting for transfers between devices  122 us (39%)
  matrix products  61.1 us (20%)
  blocking collectives  27.1 us (9%)
  starting transfers between devices  25.8 us (8%)
  local copies, waits for them, and re-layouts  24.1 us (8%)
  Pallas kernels  22.9 us (7%)
  other arithmetic  15.4 us (5%)
  between operations  14 us (4%)
    all_to_all x2, waiting for transfers between devices, layer_body(): lax.all_to_all(outgoing[:, chunk * part:(chunk + 1) * part], ('dp', 'z'),...  39.4 us
    all_to_all x2, waiting for transfers between devices, layer_body(): lax.all_to_all(total.astype(jnp.bfloat16).reshape(EXPERTS, part, D), ('dp...  37.9 us
    all_gather x1, waiting for transfers between devices, layer_body(): shard_rows = lax.all_gather(normed, HEAD, axis=0, tiled=True)  34.9 us
    all_to_all x1, blocking collectives, layer_body(): lax.all_to_all(cache_part, 'dp', split_axis=0, concat_axis=1, tiled=True)[0]  27.1 us
    dot_general x4, matrix products, expert_half(): mixed_rows = jnp.dot(rows, gate_up, preferred_element_type=jnp.float32)  24.6 us
    pallas_call x1, Pallas kernels, attend_all(): pl.pallas_call(attend_kernel, grid=(span // Q_BLOCK,), in_specs=in_specs,...  22.9 us
    unnamed x57, local copies, waits for them, and re-layouts  14.3 us
    dot_general x4, matrix products, expert_half(): jnp.dot(active, down, preferred_element_type=jnp.float32)  13.9 us
  transfers between devices with their start and end apart: 10, of which 6 were waited for; matrix products, arithmetic and copies ran while one was open for 28% of the time, Pallas kernels for 7%

commit v1 on v0

--- a/solution.py
+++ b/solution.py
@@ -60,7 +60,7 @@
     )
 
 
-Q_BLOCK = 128
+Q_BLOCK = 256
 
 
 def attend_kernel(qn_ref, qr_ref, *refs):
@@ -261,9 +261,12 @@
     )
     weights_hi = slot_weights.astype(jnp.bfloat16)
     weights_lo = (slot_weights - weights_hi.astype(jnp.float32)).astype(jnp.bfloat16)
-    routed_out = jnp.dot(weights_hi, returned, preferred_element_type=jnp.float32) + jnp.dot(
-        weights_lo, returned, preferred_element_type=jnp.float32
-    )
+    both = jnp.dot(
+        jnp.concatenate([weights_hi, weights_lo], axis=0),
+        returned,
+        preferred_element_type=jnp.float32,
+    )
+    routed_out = both[:own_rows] + both[own_rows:]
     return (hidden + routed_out).astype(jnp.bfloat16)
 
 

time: 313 us -> 309 us (0.987)
  Pallas kernels: 22.9 us -> 19.2 us
    pallas_call x1, Pallas kernels: 22.9 us -> 19.2 us  [attend_all(): pl.pallas_call(attend_kernel, grid=(span // Q_BLOCK,), in_specs=in_specs,...]
    unnamed x57 -> x59, local copies, waits for them, and re-layouts: 14.3 us -> 14 us
  transfers between devices with their start and end apart: 10 -> 10, of which waited for: 6 -> 6; matrix products, arithmetic and copies ran while one was open for 28% -> 28% of each run, Pallas kernels for 7% -> 6%
where the time goes in v1:
time: 309 us; the launch traced here: 308 us
  waiting for transfers between devices  121 us (39%)
  matrix products  60 us (19%)
  blocking collectives  27.1 us (9%)
  starting transfers between devices  26.2 us (8%)
  local copies, waits for them, and re-layouts  23.7 us (8%)
  Pallas kernels  19.2 us (6%)
  other arithmetic  16.6 us (5%)
  between operations  14 us (5%)
    all_to_all x2, waiting for transfers between devices, layer_body(): lax.all_to_all(outgoing[:, chunk * part:(chunk + 1) * part], ('dp', 'z'),...  39.1 us
    all_to_all x2, waiting for transfers between devices, layer_body(): lax.all_to_all(total.astype(jnp.bfloat16).reshape(EXPERTS, part, D), ('dp...  37.7 us
    all_gather x1, waiting for transfers between devices, layer_body(): shard_rows = lax.all_gather(normed, HEAD, axis=0, tiled=True)  34.9 us
    all_to_all x1, blocking collectives, layer_body(): lax.all_to_all(cache_part, 'dp', split_axis=0, concat_axis=1, tiled=True)[0]  27.1 us
    dot_general x4, matrix products, expert_half(): mixed_rows = jnp.dot(rows, gate_up, preferred_element_type=jnp.float32)  24.6 us
    pallas_call x1, Pallas kernels, attend_all(): pl.pallas_call(attend_kernel, grid=(span // Q_BLOCK,), in_specs=in_specs,...  19.2 us
    unnamed x59, local copies, waits for them, and re-layouts  14 us
    dot_general x4, matrix products, expert_half(): jnp.dot(active, down, preferred_element_type=jnp.float32)  13.9 us
  transfers between devices with their start and end apart: 10, of which 6 were waited for; matrix products, arithmetic and copies ran while one was open for 28% of the time, Pallas kernels for 6%

profile of v1, /device:TPU:0, one launch (start us, length us, event | category | flops | bytes accessed | tf_op | source)
XLA Modules:
  0.0 307.7 jit_solution(2394800369495722907)
XLA Ops:
  6.5 1.4 fusion.31
  7.9 2.0 fusion.33
  10.0 34.9 %all-gather.3.cloned.1.call-done = bf16[1024,2048]{1,0:T(8,128)(2,1)} async-done(((bf16[128,2048]{1,0:T(8,128)(2,1)}), bf16[1024,2048]{1,0:T(8,128)(2,1)}) %all-gather.3.cloned.1.call-update) | async-done | bytes 4194320 | tf_op jit(solution)/shard_map/all_gather | solution.py:172
  44.9 2.2 constant_dynamic-slice_fusion
  47.2 3.8 %copy.79 = bf16[16,64,576]{2,1,0:T(8,128)(2,1)} copy(bf16[16,64,576]{1,2,0:T(8,128)(2,1)} %constant_dynamic-slice_fusion) | data formatting | bytes 2359296
  51.0 27.1 %all_to_all.45 = bf16[16,64,576]{2,1,0:T(8,128)(2,1)S(1)} all-to-all(bf16[16,64,576]{2,1,0:T(8,128)(2,1)} %copy.79), channel_id=1, replica_groups=mesh['dp'=16,'z'=4,'core'=2] {'dp'}, dimensions={0} | all-to-all | bytes 2359296 | tf_op jit(solution)/shard_map/all_to_all | solution.py:183
  79.7 1.8 reduce-window.6
  83.8 2.0 convolution_convert_fusion.7.refs_0_
  85.8 0.9 slice.112
  86.9 2.2 convolution_convert_fusion.6.refs_3_
  89.1 4.6 %fusion.70 = f32[1024,576]{0,1:T(8,128)S(1)} fusion(bf16[1024,2048]{1,0:T(8,128)(2,1)} %all-gather.3.cloned.1.call-done, bf16[2048,576]{0,1:T(8,128)(2,1)S(1)} %copy-done.21), kind=kOutput, calls=%fused_computation.113 | convolution fusion | flops 2415919104 | bytes 8912896 | tf_op jit(solution)/shard_map/dot_general | solution.py:177
  93.8 1.4 copy-done.7
  95.2 1.0 copy.81
  96.2 1.0 copy.82
  97.2 4.5 %fusion.69 = f32[1024,384]{0,1:T(8,128)S(1)} fusion(bf16[1024,2048]{1,0:T(8,128)(2,1)} %all-gather.3.cloned.1.call-done, bf16[2048,384]{1,0:T(8,128)(2,1)} %param.20), kind=kOutput, calls=%fused_computation.112 | convolution fusion | flops 1610612736 | bytes 7340032 | tf_op jit(solution)/shard_map/dot_general | solution.py:49
  101.7 0.9 slice.168
  102.6 1.3 copy.77
  103.9 1.3 copy.78
  105.2 1.2 copy.72.qn_ref
  106.5 3.9 %subtract_convert_fusion.2 = (bf16[1024,32]{1,0:T(8,128)(2,1)S(1)}, bf16[1024,32]{1,0:T(8,128)(2,1)S(1)}, f32[1024,32]{1,0:T(8,128)S(1)}, f32[1024,32]{1,0:T(8,128)S(1)}) fusion(f32[1024,32]{1,0:T(8,128)} %copy.82, f32[1024,32]{1,0:T(8,128)} %copy.81, f32[1024]{0:T(1024)S(1)} %add_convert_fusion.4, f32[32]{0:T(128)S(1)} %copy-done.18), kind=kLoop, calls=%fused_computation.78 | loop fusion | flops 294912 | bytes 659584 | tf_op jit(solution)/shard_map/convert
  111.2 1.0 copy-done.8
  113.3 19.2 %shard_map.154 = bf16[1024,256]{1,0:T(8,128)(2,1)} custom-call(bf16[1024,256]{1,0:T(8,128)(2,1)S(1)} %copy.72.qn_ref, bf16[2,1024,64]{2,1,0:T(8,128)(2,1)S(1)} %maximum_bitcast_fusion.qr_ref, bf16[1024,512]{1,0:T(8,128)(2,1)S(1)} %convolution_convert_fusion.7.refs_0_, bf16[1024,64]{1,0:T(8,128)(2,1)S(1)} %slice.110.refs_1_, ...), custom_call_target="tpu_custom_call" | custom-call | tf_op jit(solution)/shard_map/pallas_call | solution.py:123
  132.5 3.7 %all-to-all-start.1 = ((bf16[8,128,256]{2,1,0:T(8,128)(2,1)}), bf16[8,128,256]{2,1,0:T(8,128)(2,1)S(1)}, u32[]{:S(2)}, u32[]{:S(2)}) async-start(bf16[8,128,256]{2,1,0:T(8,128)(2,1)} %bitcast.5), calls=%async_computation.1 | async-start | bytes 1048576 | tf_op jit(solution)/shard_map/all_to_all | solution.py:213
  137.1 9.2 %all-to-all-done.1 = bf16[8,128,256]{2,1,0:T(8,128)(2,1)S(1)} async-done(((bf16[8,128,256]{2,1,0:T(8,128)(2,1)}), bf16[8,128,256]{2,1,0:T(8,128)(2,1)S(1)}, u32[]{:S(2)}, u32[]{:S(2)}) %all-to-all-start.1) | async-done | bytes 524320 | tf_op jit(solution)/shard_map/all_to_all | solution.py:213
  146.3 4.7 %convert_reduce_fusion = f32[128,2048]{1,0:T(8,128)S(1)} fusion(bf16[8,256,2048]{2,1,0:T(8,128)(2,1)} %bitcast.86, bf16[8,128,256]{2,1,0:T(8,128)(2,1)S(1)} %all-to-all-done.1), kind=kOutput, calls=%fused_computation | convolution fusion | flops 1079771136 | bytes 9961472 | tf_op jit(solution)/shard_map/tgc,gcd->gtd/dot_general | solution.py:214
  151.3 1.3 convolution_convert_fusion
  152.6 2.5 fusion.66
  155.1 5.2 %all-to-all-start.2 = ((bf16[64,8,2048]{2,1,0:T(8,128)(2,1)}), bf16[64,8,2048]{2,1,0:T(8,128)(2,1)S(1)}, u32[]{:S(2)}, u32[]{:S(2)}) async-start(bf16[64,8,2048]{2,1,0:T(8,128)(2,1)} %get-tuple-element.11), calls=%async_computation.2 | async-start | bytes 4194304 | tf_op jit(solution)/shard_map/all_to_all | solution.py:238
  160.4 29.3 %all-to-all-done.2 = bf16[64,8,2048]{2,1,0:T(8,128)(2,1)S(1)} async-done(((bf16[64,8,2048]{2,1,0:T(8,128)(2,1)}), bf16[64,8,2048]{2,1,0:T(8,128)(2,1)S(1)}, u32[]{:S(2)}, u32[]{:S(2)}) %all-to-all-start.2) | async-done | bytes 2097184 | tf_op jit(solution)/shard_map/all_to_all | solution.py:238
  189.7 1.3 copy-done.11
  191.0 5.5 %all-to-all-start.4 = ((bf16[64,8,2048]{2,1,0:T(8,128)(2,1)}), bf16[64,8,2048]{2,1,0:T(8,128)(2,1)S(1)}, u32[]{:S(2)}, u32[]{:S(2)}) async-start(bf16[64,8,2048]{2,1,0:T(8,128)(2,1)} %get-tuple-element.12), calls=%async_computation.4 | async-start | bytes 4194304 | tf_op jit(solution)/shard_map/all_to_all | solution.py:238
  196.5 6.5 %fusion.6 = f32[512,1408]{1,0:T(8,128)S(1)} fusion(bf16[1,2048,1408]{2,1,0:T(8,128)(2,1)} %param.28, bf16[64,8,2048]{2,1,0:T(8,128)(2,1)} %copy-done.11), kind=kOutput, calls=%fused_computation.7 | convolution fusion | flops 2952790016 | bytes 10747904 | tf_op jit(solution)/shard_map/dot_general | solution.py:137
  203.1 1.9 convolution_convert_fusion.4
  205.0 5.7 %fusion.2 = f32[512,1408]{1,0:T(8,128)S(1)} fusion(bf16[1,2048,1408]{2,1,0:T(8,128)(2,1)} %collective-permute-done.1, bf16[64,8,2048]{2,1,0:T(8,128)(2,1)S(1)} %copy-done.12), kind=kOutput, calls=%fused_computation.3 | convolution fusion | flops 2952790016 | bytes 10747904 | tf_op jit(solution)/shard_map/dot_general | solution.py:137
  210.8 5.0 %fusion.15 = bf16[64,8,2048]{2,1,0:T(8,128)(2,1)} fusion(bf16[1,704,2048]{2,1,0:T(8,128)(2,1)} %collective-permute-done.2, bf16[512,2048]{1,0:T(8,128)(2,1)S(1)} %convolution_convert_fusion.4, f32[512,1408]{1,0:T(8,128)S(1)} %fusion.2), kind=kOutput, calls=%fused_computation.25 | convolution fusion | flops 1483800576 | bytes 10223616 | tf_op jit(solution)/shard_map/dot_general | solution.py:140
  215.8 9.8 %all-to-all-done.4 = bf16[64,8,2048]{2,1,0:T(8,128)(2,1)S(1)} async-done(((bf16[64,8,2048]{2,1,0:T(8,128)(2,1)}), bf16[64,8,2048]{2,1,0:T(8,128)(2,1)S(1)}, u32[]{:S(2)}, u32[]{:S(2)}) %all-to-all-start.4) | async-done | bytes 2097184 | tf_op jit(solution)/shard_map/all_to_all | solution.py:238
  225.7 1.4 copy-done.9
  227.0 5.6 %all-to-all-start.3 = ((bf16[64,8,2048]{2,1,0:T(8,128)(2,1)}), bf16[64,8,2048]{2,1,0:T(8,128)(2,1)S(1)}, u32[]{:S(2)}, u32[]{:S(2)}) async-start(bf16[64,8,2048]{2,1,0:T(8,128)(2,1)} %fusion.15), calls=%async_computation.3 | async-start | bytes 4194304 | tf_op jit(solution)/shard_map/all_to_all | solution.py:249
  232.6 6.5 %fusion.4 = f32[512,1408]{1,0:T(8,128)S(1)} fusion(bf16[1,2048,1408]{2,1,0:T(8,128)(2,1)} %param.28, bf16[64,8,2048]{2,1,0:T(8,128)(2,1)} %copy-done.9), kind=kOutput, calls=%fused_computation.5 | convolution fusion | flops 2952790016 | bytes 10747904 | tf_op jit(solution)/shard_map/dot_general | solution.py:137
  239.2 1.9 convolution_convert_fusion.2
  241.1 5.7 %fusion = f32[512,1408]{1,0:T(8,128)S(1)} fusion(bf16[1,2048,1408]{2,1,0:T(8,128)(2,1)} %collective-permute-done.1, bf16[64,8,2048]{2,1,0:T(8,128)(2,1)S(1)} %copy-done.10), kind=kOutput, calls=%fused_computation.1 | convolution fusion | flops 2952790016 | bytes 10747904 | tf_op jit(solution)/shard_map/dot_general | solution.py:137
  246.8 5.1 %fusion.20 = bf16[64,8,2048]{2,1,0:T(8,128)(2,1)} fusion(bf16[1,704,2048]{2,1,0:T(8,128)(2,1)} %collective-permute-done.2, bf16[512,2048]{1,0:T(8,128)(2,1)S(1)} %convolution_convert_fusion.2, f32[512,1408]{1,0:T(8,128)S(1)} %fusion), kind=kOutput, calls=%fused_computation.26 | convolution fusion | flops 1483800576 | bytes 10223616 | tf_op jit(solution)/shard_map/dot_general | solution.py:140
  251.9 9.8 %all-to-all-done.3 = bf16[64,8,2048]{2,1,0:T(8,128)(2,1)S(1)} async-done(((bf16[64,8,2048]{2,1,0:T(8,128)(2,1)}), bf16[64,8,2048]{2,1,0:T(8,128)(2,1)S(1)}, u32[]{:S(2)}, u32[]{:S(2)}) %all-to-all-start.3) | async-done | bytes 2097184 | tf_op jit(solution)/shard_map/all_to_all | solution.py:249
  261.7 5.6 %all-to-all-start.5 = ((bf16[64,8,2048]{2,1,0:T(8,128)(2,1)}), bf16[64,8,2048]{2,1,0:T(8,128)(2,1)}, u32[]{:S(2)}, u32[]{:S(2)}) async-start(bf16[64,8,2048]{2,1,0:T(8,128)(2,1)} %fusion.20), calls=%async_computation.5 | async-start | bytes 4194304 | tf_op jit(solution)/shard_map/all_to_all | solution.py:249
  268.6 27.9 %all-to-all-done.5 = bf16[64,8,2048]{2,1,0:T(8,128)(2,1)} async-done(((bf16[64,8,2048]{2,1,0:T(8,128)(2,1)}), bf16[64,8,2048]{2,1,0:T(8,128)(2,1)}, u32[]{:S(2)}, u32[]{:S(2)}) %all-to-all-start.5) | async-done | bytes 2097184 | tf_op jit(solution)/shard_map/all_to_all | solution.py:249
  296.4 2.0 pad_maximum_fusion
  298.4 1.3 fusion.48
  299.7 1.1 fusion.35
  (90 shorter events, 8.4 us)
Async XLA Ops:
  6.5 38.4 %copy-start = (bf16[16,128,576]{1,2,0:T(8,128)(2,1)S(1)}, bf16[16,128,576]{1,2,0:T(8,128)(2,1)}, u32[]{:S(2)}) copy-start(bf16[16,128,576]{1,2,0:T(8,128)(2,1)} %param.18) | copy-start | bytes 7077892
  6.5 38.4 %all-gather.3.cloned.1.call-start = ((), (), s32[]{:S(2)}) async-start(), calls=%async_computation.6 | async-start | bytes 4718592 | tf_op jit(solution)/shard_map/all_gather | solution.py:172
  10.0 136.3 %all-gather.5.cloned.1.call-start = ((), (), s32[]{:S(2)}) async-start(), calls=%async_computation.7 | async-start | bytes 9437184 | tf_op jit(solution)/shard_map/all_gather | solution.py:174
  51.0 28.3 %copy-start.15 = (s32[128,6]{0,1:T(8,128)S(1)}, s32[128,6]{0,1:T(8,128)}, u32[]{:S(2)}) copy-start(s32[128,6]{0,1:T(8,128)} %param.26) | copy-start | bytes 9220
  78.0 5.7 %copy-start.4 = (bf16[16,64,576]{2,1,0:T(8,128)(2,1)}, bf16[16,64,576]{2,1,0:T(8,128)(2,1)S(1)}, u32[]{:S(2)}) copy-start(bf16[16,64,576]{2,1,0:T(8,128)(2,1)S(1)} %all_to_all.45) | copy-start | bytes 3538948
  78.1 3.7 %copy-start.25 = (s32[16]{0:T(128)S(1)}, s32[16]{0:T(128)}, u32[]{:S(2)}) copy-start(s32[16]{0:T(128)} %param.17) | copy-start | bytes 196
  78.1 5.7 %copy-start.22 = (bf16[512,512]{1,0:T(8,128)(2,1)S(1)}, bf16[512,512]{1,0:T(8,128)(2,1)}, u32[]{:S(2)}) copy-start(bf16[512,512]{1,0:T(8,128)(2,1)} %param.23) | copy-start | bytes 1572868
  78.7 7.1 %collective-permute-start = (bf16[1024,576]{0,1:T(8,128)(2,1)S(1)}, bf16[1024,576]{0,1:T(8,128)(2,1)}, u32[]{:S(2)}, u32[]{:S(2)}) collective-permute-start(bf16[1024,576]{0,1:T(8,128)(2,1)S(1)} %copy.68), channel_id=1, source_target_pairs={{0,1},{1,0},{2,3},{3,2},{4,5},{5,4},{6,7},{7,6},{8,9},{9,8},{10,11... | collective-permute-start | bytes 3538952 | tf_op jit(solution)/shard_map/ppermute | solution.py:190
  78.8 126.2 %collective-permute-start.1 = (bf16[1,2048,1408]{2,1,0:T(8,128)(2,1)}, bf16[1,2048,1408]{2,1,0:T(8,128)(2,1)}, u32[]{:S(2)}, u32[]{:S(2)}) collective-permute-start(bf16[1,2048,1408]{2,1,0:T(8,128)(2,1)} %param.28), channel_id=1, source_target_pairs={{0,1},{1,0},{2,3},{3,2},{4,5},{5,4},{6,7},{7,6},{8,9},{9,8},{10,11... | collective-permute-start | bytes 17301512 | tf_op jit(solution)/shard_map/ppermute | solution.py:164
  86.9 2.3 copy-start.21
  93.7 1.4 copy-start.7
  102.5 3.9 %copy-start.18 = (f32[32]{0:T(128)S(1)}, f32[32]{0:T(128)}, u32[]{:S(2)}) copy-start(f32[32]{0:T(128)} %constant.83.clone) | copy-start | bytes 388
  106.5 4.1 %copy-start.5 = (f32[1024,2,32]{2,0,1:T(8,128)S(1)}, f32[1024,2,32]{2,0,1:T(8,128)}, u32[]{:S(2)}) copy-start(f32[1024,2,32]{2,0,1:T(8,128)} %copy.77) | copy-start | bytes 786436
  106.5 4.1 %copy-start.6 = (f32[1024,2,32]{2,0,1:T(8,128)S(1)}, f32[1024,2,32]{2,0,1:T(8,128)}, u32[]{:S(2)}) copy-start(f32[1024,2,32]{2,0,1:T(8,128)} %copy.78) | copy-start | bytes 786436
  110.6 1.7 copy-start.8
  110.8 1.6 copy-start.23
  110.9 1.6 copy-start.24
  132.5 13.7 %all-to-all-start.1 = ((bf16[8,128,256]{2,1,0:T(8,128)(2,1)}), bf16[8,128,256]{2,1,0:T(8,128)(2,1)S(1)}, u32[]{:S(2)}, u32[]{:S(2)}) async-start(bf16[8,128,256]{2,1,0:T(8,128)(2,1)} %bitcast.5), calls=%async_computation.1 | async-start | bytes 1048576 | tf_op jit(solution)/shard_map/all_to_all | solution.py:213
  146.3 4.8 %copy-start.2 = (bf16[128,2048]{1,0:T(8,128)(2,1)S(1)}, bf16[128,2048]{1,0:T(8,128)(2,1)}, u32[]{:S(2)}) copy-start(bf16[128,2048]{1,0:T(8,128)(2,1)} %param.16) | copy-start | bytes 1572868
  146.3 5.0 %copy-start.16 = (f32[2048]{0:T(1024)S(1)}, f32[2048]{0:T(1024)}, u32[]{:S(2)}) copy-start(f32[2048]{0:T(1024)} %param.25) | copy-start | bytes 24580
  155.1 34.6 %all-to-all-start.2 = ((bf16[64,8,2048]{2,1,0:T(8,128)(2,1)}), bf16[64,8,2048]{2,1,0:T(8,128)(2,1)S(1)}, u32[]{:S(2)}, u32[]{:S(2)}) async-start(bf16[64,8,2048]{2,1,0:T(8,128)(2,1)} %get-tuple-element.11), calls=%async_computation.2 | async-start | bytes 4194304 | tf_op jit(solution)/shard_map/all_to_all | solution.py:238
  160.3 50.5 %collective-permute-start.2 = (bf16[1,704,2048]{2,1,0:T(8,128)(2,1)}, bf16[1,704,2048]{2,1,0:T(8,128)(2,1)}, u32[]{:S(2)}, u32[]{:S(2)}) collective-permute-start(bf16[1,704,2048]{2,1,0:T(8,128)(2,1)} %param.29), channel_id=1, source_target_pairs={{0,1},{1,0},{2,3},{3,2},{4,5},{5,4},{6,7},{7,6},{8,9},{9,8},{10,11... | collective-permute-start | bytes 8650760 | tf_op jit(solution)/shard_map/ppermute | solution.py:165
  189.7 1.3 copy-start.11
  191.0 34.6 %all-to-all-start.4 = ((bf16[64,8,2048]{2,1,0:T(8,128)(2,1)}), bf16[64,8,2048]{2,1,0:T(8,128)(2,1)S(1)}, u32[]{:S(2)}, u32[]{:S(2)}) async-start(bf16[64,8,2048]{2,1,0:T(8,128)(2,1)} %get-tuple-element.12), calls=%async_computation.4 | async-start | bytes 4194304 | tf_op jit(solution)/shard_map/all_to_all | solution.py:238
  196.5 6.6 %copy-start.19 = (bf16[1,704,2048]{2,1,0:T(8,128)(2,1)S(1)}, bf16[1,704,2048]{2,1,0:T(8,128)(2,1)}, u32[]{:S(2)}) copy-start(bf16[1,704,2048]{2,1,0:T(8,128)(2,1)} %param.29) | copy-start | bytes 8650756
  203.1 1.9 copy-start.12
  225.7 1.4 copy-start.9
  227.0 34.7 %all-to-all-start.3 = ((bf16[64,8,2048]{2,1,0:T(8,128)(2,1)}), bf16[64,8,2048]{2,1,0:T(8,128)(2,1)S(1)}, u32[]{:S(2)}, u32[]{:S(2)}) async-start(bf16[64,8,2048]{2,1,0:T(8,128)(2,1)} %fusion.15), calls=%async_computation.3 | async-start | bytes 4194304 | tf_op jit(solution)/shard_map/all_to_all | solution.py:249
  232.6 6.6 %copy-start.20 = (bf16[1,704,2048]{2,1,0:T(8,128)(2,1)S(1)}, bf16[1,704,2048]{2,1,0:T(8,128)(2,1)}, u32[]{:S(2)}) copy-start(bf16[1,704,2048]{2,1,0:T(8,128)(2,1)} %param.29) | copy-start | bytes 8650756
  239.2 1.9 copy-start.10
  251.9 15.4 %copy-start.17 = (f32[128,6]{0,1:T(8,128)S(1)}, f32[128,6]{0,1:T(8,128)}, u32[]{:S(2)}) copy-start(f32[128,6]{0,1:T(8,128)} %param.27) | copy-start | bytes 9220
  261.7 34.7 %all-to-all-start.5 = ((bf16[64,8,2048]{2,1,0:T(8,128)(2,1)}), bf16[64,8,2048]{2,1,0:T(8,128)(2,1)}, u32[]{:S(2)}, u32[]{:S(2)}) async-start(bf16[64,8,2048]{2,1,0:T(8,128)(2,1)} %fusion.20), calls=%async_computation.5 | async-start | bytes 4194304 | tf_op jit(solution)/shard_map/all_to_all | solution.py:249
  296.4 2.0 copy-start.13
  296.4 2.0 copy-start.14
  298.4 1.3 copy-start.3
  298.4 2.4 copy-start.1
Sparse Core Ops, SparseCore 0:
  10.1 34.7 all-gather.2
  46.6 49.6 all-gather.4
